TPU v7x, 32 devices: a whole 2x2x4 slice. The times are simulated.
32 devices in a mesh: groups: 2 (over y), replica: 4 (over z), tensor: 4 (over x, core).
Axes of the slice: x: 2, y: 2, z: 4, core: 2. Of those that a mesh axis runs over, the one named last changes fastest.
Arguments:
- queries: bfloat16 [8, 128, 8192], P(('groups', 'replica'), None, 'tensor'), parts along dimension 0, may hold values from -12 to 12
- suffix_kv: bfloat16 [8, 2, 128, 1024], P(('groups', 'replica'), None, None, 'tensor'), parts along dimension 0, may hold values from -12 to 12
- page_pool: bfloat16 [96, 2, 128, 1024], P(('groups', 'replica'), None, 'tensor'), parts along dimension 0, may hold values from -6 to 6
- offsets: int32 [8, 8], P('groups'), parts along dimension 0, may hold values from 1 to 3, as said below
- slots: int32 [8, 8], P('groups'), parts along dimension 0, may hold values from 0 to 11, as said below
- prefix_len: int32 [8], P('groups'), parts along dimension 0, may hold values from 1 to 1024, 2048 in all
Outputs:
- attended: bfloat16 [8, 128, 8192], P(('groups', 'replica'), None, 'tensor'), parts along dimension 0
There are 2 independent parts, one for each index of `groups`. A program takes and returns all parts, laid end to end along the dimension named above; each array names one. Nothing has to cross between parts.
Inputs may be any that keep to these rules, and one draw needn't show every extreme that they name: Page p of request r is held by replica (r - offsets[r, p]) mod 4; one request takes at most 4 pages from one holder, and exactly 4 from some holder. `slots`: the prefix pages of one request are distinct pool entries. `prefix_len`: the longest prefix fills all 8 pages.
All inputs are finite; a program needn't handle non-finite values.
Results may differ from a plain program's by a relative error of at most 0.0034.
Values may be sent and summed in bfloat16 or wider, within the bound.
No kernel may reach another device: no remote copies, remote signals or barrier semaphores. Data moves between devices by JAX's collectives and lax.ppermute only.
A program may use at most 64 MiB of HBM per device.

v0:
```python
import math
import jax
import jax.numpy as jnp
from jax import lax
from jax.sharding import PartitionSpec as P

HEADS = 64
KV_HEADS = 8
HEAD_DIM = 128
NEG_FILL = -1e30


def passed_along(value, axis, steps):
    count = lax.axis_size(axis)
    pairs = [(source, (source + steps) % count) for source in range(count)]
    return lax.ppermute(value, axis, pairs)


def absorb(state_now, scores, visible, values):
    run_max, run_sum, run_acc = state_now
    masked = jnp.where(visible, scores, NEG_FILL)
    new_max = jnp.maximum(run_max, jnp.max(masked, axis=-1))
    weights = jnp.where(visible, jnp.exp(masked - new_max[..., None]), 0.0)
    rescale = jnp.exp(run_max - new_max)
    run_sum = run_sum * rescale + jnp.sum(weights, axis=-1)
    update = jnp.einsum(
        "kgqc,ckd->kgqd", weights.astype(jnp.bfloat16), values, preferred_element_type=jnp.float32
    )
    run_acc = run_acc * rescale[..., None] + update
    return (new_max, run_sum, run_acc)


def pack_pages(pool_part, offsets, slots, holder, replicas, span_count, slot_cap):
    distances = jnp.arange(1, span_count + 1, dtype=jnp.int32)
    readers = (holder + distances) % replicas
    off_rows = jnp.take(offsets, readers, axis=0)
    slot_rows = jnp.take(slots, readers, axis=0)
    matched = (off_rows == distances[:, None]).astype(jnp.int32)
    ranking = jnp.cumsum(matched, axis=1) - 1
    places = jnp.arange(slot_cap, dtype=jnp.int32)
    picked = matched[:, None, :] * (ranking[:, None, :] == places[None, :, None]).astype(jnp.int32)
    chosen = jnp.sum(picked * slot_rows[:, None, :], axis=2)
    gathered = jnp.take(pool_part, chosen.reshape(-1), axis=0)
    return gathered.reshape((span_count, slot_cap) + pool_part.shape[1:])


def page_index(own_offsets, slot_cap):
    page_count = own_offsets.shape[0]
    same_holder = own_offsets[:, None] == own_offsets[None, :]
    counter = jnp.arange(page_count, dtype=jnp.int32)
    earlier = counter[None, :] < counter[:, None]
    ranking = jnp.sum((same_holder & earlier).astype(jnp.int32), axis=1)
    return (own_offsets - 1) * slot_cap + ranking


def on_device(queries, suffix_kv, page_pool, offsets, slots, prefix_len):
    replicas = lax.axis_size("replica")
    reader = lax.axis_index("replica")
    span_count = min(8, replicas - 1)
    page_count = offsets.shape[1]
    slot_cap = (page_count + span_count - 1) // span_count + 1
    own_offsets = lax.dynamic_index_in_dim(offsets, reader, 0, keepdims=False)
    own_length = lax.dynamic_index_in_dim(prefix_len, reader, 0, keepdims=False)
    source = lax.all_to_all(page_pool, "tensor", split_axis=3, concat_axis=2, tiled=True)
    payload = pack_pages(source, offsets, slots, reader, replicas, span_count, slot_cap)
    arrivals = []
    for distance in range(1, span_count + 1):
        arrivals.append(passed_along(payload[distance - 1], "replica", distance))
    arrived = jnp.stack(arrivals)
    flattened = arrived.reshape((span_count * slot_cap,) + arrived.shape[2:])
    fetched = jnp.take(flattened, page_index(own_offsets, slot_cap), axis=0)
    width = fetched.shape[3]
    kv_local = width // HEAD_DIM
    group = HEADS // KV_HEADS
    suffix_rows = queries.shape[1]
    prefix_rows = page_count * fetched.shape[2]
    scale = HEAD_DIM ** (-0.5)
    query_heads = queries[0].reshape(suffix_rows, kv_local, group, HEAD_DIM)
    suffix_keys = suffix_kv[0, 0].reshape(suffix_rows, kv_local, HEAD_DIM)
    suffix_vals = suffix_kv[0, 1].reshape(suffix_rows, kv_local, HEAD_DIM)
    initial = (
        jnp.full((kv_local, group, suffix_rows), NEG_FILL, jnp.float32),
        jnp.zeros((kv_local, group, suffix_rows), jnp.float32),
        jnp.zeros((kv_local, group, suffix_rows, HEAD_DIM), jnp.float32),
    )
    suffix_scores = (
        jnp.einsum("qkgd,ckd->kgqc", query_heads, suffix_keys, preferred_element_type=jnp.float32)
        * scale
    )
    query_pos = jnp.arange(suffix_rows, dtype=jnp.int32)
    causal = query_pos[:, None] >= query_pos[None, :]
    state_now = absorb(initial, suffix_scores, causal, suffix_vals)
    block_rows = math.gcd(prefix_rows, 512)
    block_count = prefix_rows // block_rows
    prefix_keys = fetched[:, 0].reshape(block_count, block_rows, kv_local, HEAD_DIM)
    prefix_vals = fetched[:, 1].reshape(block_count, block_rows, kv_local, HEAD_DIM)
    block_pos = jnp.arange(block_rows, dtype=jnp.int32)

    def visit(state_in, pieces):
        keys_block, vals_block, first_row = pieces
        block_scores = (
            jnp.einsum(
                "qkgd,ckd->kgqc", query_heads, keys_block, preferred_element_type=jnp.float32
            )
            * scale
        )
        visible = first_row + block_pos < own_length
        return (absorb(state_in, block_scores, visible, vals_block), None)

    starts = jnp.arange(block_count, dtype=jnp.int32) * block_rows
    state_now, unused = lax.scan(visit, state_now, (prefix_keys, prefix_vals, starts))
    run_max, run_sum, run_acc = state_now
    result = run_acc / run_sum[..., None]
    result = result.transpose(2, 0, 1, 3).reshape(1, suffix_rows, kv_local * group * HEAD_DIM)
    return result.astype(jnp.bfloat16)


def solution(mesh):
    in_specs = (
        P(("groups", "replica"), None, "tensor"),
        P(("groups", "replica"), None, None, "tensor"),
        P(("groups", "replica"), None, "tensor", None),
        P("groups", None),
        P("groups", None),
        P("groups"),
    )
    out_specs = P(("groups", "replica"), None, "tensor")
    return jax.shard_map(
        on_device, mesh=mesh, in_specs=in_specs, out_specs=out_specs, check_vma=False
    )
```

profile of v0, /device:TPU:9, one launch (start us, length us, event | category | flops | bytes accessed | tf_op | source)
XLA Modules:
  0.0 132.8 jit_solution(631455684307266697)
XLA Ops:
  0.0 12.7 %copy.73 = bf16[12,2,32,1024]{2,0,1,3:T(8,128)(2,1)} copy(bf16[12,2,32,1024]{3,2,1,0:T(8,128)(2,1)} %param.12) | data formatting | bytes 3145728 | tf_op args[2]
  12.7 8.9 %reshape.178 = bf16[4,2,98304]{2,1,0:T(2,128)(2,1)} reshape(bf16[1024,2,12,32]{3,2,1,0:T(8,128)(2,1)} %bitcast.95) | data formatting | bytes 3145728
  21.6 4.3 %all-to-all-start = ((bf16[4,2,98304]{2,1,0:T(2,128)(2,1)}), bf16[4,2,98304]{2,1,0:T(2,128)(2,1)S(1)}, u32[]{:S(2)}, u32[]{:S(2)}) async-start(bf16[4,2,98304]{2,1,0:T(2,128)(2,1)} %reshape.178), calls=%async_computation | async-start | bytes 3145728 | tf_op jit(solution)/shard_map/all_to_all | solution.py:64
  26.0 0.6 gather_fusion.2
  26.5 0.6 gather_fusion.3
  27.2 0.2 reduce_window_sum.11
  27.4 0.1 multiply_reduce_fusion
  27.8 0.2 convert_reduce_fusion
  28.0 0.3 copy.67
  28.4 0.4 fusion.38
  28.8 0.2 fusion.21
  29.1 16.0 %all-to-all-done = bf16[4,2,98304]{2,1,0:T(2,128)(2,1)S(1)} async-done(((bf16[4,2,98304]{2,1,0:T(2,128)(2,1)}), bf16[4,2,98304]{2,1,0:T(2,128)(2,1)S(1)}, u32[]{:S(2)}, u32[]{:S(2)}) %all-to-all-start) | async-done | bytes 1572896 | tf_op jit(solution)/shard_map/all_to_all | solution.py:64
  45.1 7.1 %reshape.179 = bf16[1024,2,12,32]{3,2,1,0:T(8,128)(2,1)} reshape(bf16[4,2,98304]{2,1,0:T(2,128)(2,1)S(1)} %all-to-all-done) | data formatting | bytes 3145728
  52.2 9.6 %copy.91 = bf16[12,2,32,4,256]{4,3,2,1,0:T(4,128)(2,1)S(1)} copy(bf16[12,2,32,4,256]{2,0,1,4,3:T(8,128)(2,1)} %bitcast.94) | data formatting | bytes 3145728 | tf_op jit(solution)/shard_map/all_to_all | solution.py:64
  61.7 1.5 %copy.75 = bf16[12,2,4,32,256]{4,3,2,1,0:T(8,128)(2,1)} copy(bf16[12,2,4,32,256]{4,2,3,1,0:T(4,128)(2,1)S(1)} %bitcast.96) | data formatting | bytes 3145728 | tf_op jit(solution)/shard_map/all_to_all | solution.py:64
  63.2 2.1 %gather_fusion = bf16[12,2,128,256]{3,2,1,0:T(8,128)(2,1)S(1)} fusion(bf16[12,2,128,256]{3,2,1,0:T(8,128)(2,1)} %bitcast.97, s32[1024]{0:T(1024)S(1)} %pad_clamp_fusion.1), kind=kCustom, calls=%fused_computation.2 | custom fusion | bytes 3145776 | tf_op jit(solution)/shard_map/jit(_take)/gather | solution.py:43
  65.3 0.2 broadcast_select_fusion
  65.5 1.1 fusion.35
  66.6 1.3 collective-permute-start
  67.9 1.0 collective-permute-start.1
  68.9 1.5 %collective-permute-start.2 = (bf16[4,2,128,256]{3,2,1,0:T(8,128)(2,1)S(1)}, bf16[4,2,128,256]{3,2,1,0:T(8,128)(2,1)}, u32[]{:S(2)}, u32[]{:S(2)}) collective-permute-start(bf16[4,2,128,256]{3,2,1,0:T(8,128)(2,1)S(1)} %get-tuple-element.151), channel_id=1, source_target_pairs={{0,12},{4,0},{8,4},{12,8},{1,13},{5,1},{9,5},{13,9},{2,14},{6,2},{... | collective-permute-start | bytes 1572872 | tf_op jit(solution)/shard_map/ppermute | solution.py:16
  70.4 0.3 copy.77
  70.8 0.6 dynamic_slice.19
  71.4 1.5 %convolution_add_fusion = f32[2,8,128,128]{3,2,1,0:T(8,128)} fusion(bf16[128,2,128,1]{0,2,3,1:T(8,128)(2,1)S(1)} %bitcast.102, f32[2,8,128,128]{2,3,1,0:T(8,128)S(1)} %get-tuple-element.160, f32[2,8,128]{2,1,0:T(8,128)S(1)} %get-tuple-element.157, f32[2,8,128]{2,1,0:T(8,128)S(1)} %broadcast_maximum_fusion, pred[128,128]{0,1:T(8,128)(4,1)S(1)} %iota_compare_fusion), kind=kOutput, calls=%fused_computation.30 | convolution fusion | flops 68157440 | bytes 2195456 | tf_op jit(solution)/shard_map/kgqc,ckd->kgqd/dot_general | solution.py:26
  72.9 6.5 %collective-permute-done = bf16[4,2,128,256]{3,2,1,0:T(8,128)(2,1)S(1)} collective-permute-done((bf16[4,2,128,256]{3,2,1,0:T(8,128)(2,1)}, bf16[4,2,128,256]{3,2,1,0:T(8,128)(2,1)S(1)}, u32[]{:S(2)}, u32[]{:S(2)}) %collective-permute-start) | collective-permute-done | bytes 524320 | tf_op jit(solution)/shard_map/ppermute | solution.py:16
  79.4 32.9 %collective-permute-done.1 = bf16[4,2,128,256]{3,2,1,0:T(8,128)(2,1)} collective-permute-done((bf16[4,2,128,256]{3,2,1,0:T(8,128)(2,1)}, bf16[4,2,128,256]{3,2,1,0:T(8,128)(2,1)}, u32[]{:S(2)}, u32[]{:S(2)}) %collective-permute-start.1) | collective-permute-done | bytes 524320 | tf_op jit(solution)/shard_map/ppermute | solution.py:16
  112.3 3.1 %collective-permute-done.2 = bf16[4,2,128,256]{3,2,1,0:T(8,128)(2,1)} collective-permute-done((bf16[4,2,128,256]{3,2,1,0:T(8,128)(2,1)S(1)}, bf16[4,2,128,256]{3,2,1,0:T(8,128)(2,1)}, u32[]{:S(2)}, u32[]{:S(2)}) %collective-permute-start.2) | collective-permute-done | bytes 524320 | tf_op jit(solution)/shard_map/ppermute | solution.py:16
  115.4 1.5 %pad_maximum_fusion = bf16[3,4,2,128,256]{4,3,2,1,0:T(8,128)(2,1)S(1)} fusion(bf16[1,4,2,128,256]{4,3,2,1,0:T(8,128)(2,1)} %bitcast.14, bf16[1,4,2,128,256]{4,3,2,1,0:T(8,128)(2,1)} %bitcast.13, bf16[1,4,2,128,256]{4,3,2,1,0:T(8,128)(2,1)} %bitcast.101), kind=kLoop, calls=%fused_computation.28 | loop fusion | flops 1572864 | bytes 3145728 | tf_op jit(solution)/shard_map/stack | solution.py:69
  116.9 0.6 gather_fusion.1
  117.5 0.2 broadcast_select_fusion.1
  117.8 0.1 reshape_squeeze.18
  118.1 0.8 copy-done.1
  118.9 12.1 %while.15 = (s32[]{:T(128)}, f32[2,8,128]{2,1,0:T(8,128)S(1)}, f32[2,8,128]{2,1,0:T(8,128)S(1)}, f32[2,8,128,128]{3,2,1,0:T(8,128)S(1)}, s32[2]{0:T(128)S(1)}, /...) while((s32[]{:T(128)}, f32[2,8,128]{2,1,0:T(8,128)S(1)}, ...), condition=%wide.region_8.10_spmd.clone, body=%wide.region_5.9_spmd.clone.sunk | while | flops 551031808 | bytes 16910460 | solution.py:111
  118.9 0.6 dynamic_slice.36
  119.5 1.2 fusion.50
  120.7 0.4 constant_dynamic-slice_fusion.4
  121.1 0.8 bitcast_reduce_fusion.2
  121.9 1.1 fusion.51
  123.1 1.9 %fusion.52 = f32[2,8,128,128]{3,2,1,0:T(8,128)S(1)} fusion(f32[2,512,128,8]{2,1,3,0:T(8,128)S(1)} %get-tuple-element.226, f32[2,8,128]{2,1,0:T(8,128)S(1)} %max.5, pred[512]{0:T(512)(128)(4,1)S(1)} %fusion.50, f32[2,8,128,128]{3,2,1,0:T(8,128)S(1)} %get-tuple-element.243, f32[2,8,128]{2,1,0:T(8,128)S(1)} %get-tuple-element.228, ...), kind=kOutput, calls=%fused_computation.15.clone.1 | convolution fusion | flops 274202624 | bytes 6570496 | tf_op jit(solution)/shard_map/while/body/eval_jaxpr/kgqc,ckd->kgqd/dot_general | solution.py:26
  125.0 0.6 dynamic_slice.36
  125.6 1.2 fusion.50
  126.8 0.4 constant_dynamic-slice_fusion.4
  127.2 0.8 bitcast_reduce_fusion.2
  127.9 1.1 fusion.51
  129.1 1.9 %fusion.52 = f32[2,8,128,128]{3,2,1,0:T(8,128)S(1)} fusion(f32[2,512,128,8]{2,1,3,0:T(8,128)S(1)} %get-tuple-element.226, f32[2,8,128]{2,1,0:T(8,128)S(1)} %max.5, pred[512]{0:T(512)(128)(4,1)S(1)} %fusion.50, f32[2,8,128,128]{3,2,1,0:T(8,128)S(1)} %get-tuple-element.243, f32[2,8,128]{2,1,0:T(8,128)S(1)} %get-tuple-element.228, ...), kind=kOutput, calls=%fused_computation.15.clone.1 | convolution fusion | flops 274202624 | bytes 6570496 | tf_op jit(solution)/shard_map/while/body/eval_jaxpr/kgqc,ckd->kgqd/dot_general | solution.py:26
  131.0 0.3 fusion.25
  131.4 0.3 copy.79
  131.7 1.0 convert_element_type.35
  (43 shorter events, 1.0 us)
Async XLA Ops:
  0.0 26.5 %copy-start = (s32[4,8]{1,0:T(4,128)S(1)}, s32[4,8]{1,0:T(4,128)}, u32[]{:S(2)}) copy-start(s32[4,8]{1,0:T(4,128)} %param.14) | copy-start | bytes 388
  12.7 13.3 %copy-start.4 = (s32[4,8]{1,0:T(4,128)S(1)}, s32[4,8]{1,0:T(4,128)}, u32[]{:S(2)}) copy-start(s32[4,8]{1,0:T(4,128)} %param.13) | copy-start | bytes 388
  12.7 15.3 %copy-start.2 = (bf16[1,128,2048]{2,1,0:T(8,128)(2,1)S(1)}, bf16[1,128,2048]{2,1,0:T(8,128)(2,1)}, u32[]{:S(2)}) copy-start(bf16[1,128,2048]{2,1,0:T(8,128)(2,1)} %param.10) | copy-start | bytes 1572868
  21.6 6.7 %copy-start.5 = (bf16[1,2,128,256]{3,2,1,0:T(8,128)(2,1)S(1)}, bf16[1,2,128,256]{3,2,1,0:T(8,128)(2,1)}, u32[]{:S(2)}) copy-start(bf16[1,2,128,256]{3,2,1,0:T(8,128)(2,1)} %param.11) | copy-start | bytes 393220
  21.6 23.6 %all-to-all-start = ((bf16[4,2,98304]{2,1,0:T(2,128)(2,1)}), bf16[4,2,98304]{2,1,0:T(2,128)(2,1)S(1)}, u32[]{:S(2)}, u32[]{:S(2)}) async-start(bf16[4,2,98304]{2,1,0:T(2,128)(2,1)} %reshape.178), calls=%async_computation | async-start | bytes 3145728 | tf_op jit(solution)/shard_map/all_to_all | solution.py:64
  65.3 5.5 %copy-start.6 = (s32[4]{0:T(128)S(1)}, s32[4]{0:T(128)}, u32[]{:S(2)}) copy-start(s32[4]{0:T(128)} %param.15) | copy-start | bytes 52
  66.6 12.8 %collective-permute-start = (bf16[4,2,128,256]{3,2,1,0:T(8,128)(2,1)}, bf16[4,2,128,256]{3,2,1,0:T(8,128)(2,1)S(1)}, u32[]{:S(2)}, u32[]{:S(2)}) collective-permute-start(bf16[4,2,128,256]{3,2,1,0:T(8,128)(2,1)} %get-tuple-element.150), channel_id=1, source_target_pairs={{0,4},{4,8},{8,12},{12,0},{1,5},{5,9},{9,13},{13,1},{2,6},{6,10},{... | collective-permute-start | bytes 1572872 | tf_op jit(solution)/shard_map/ppermute | solution.py:16
  67.9 44.4 %collective-permute-start.1 = (bf16[4,2,128,256]{3,2,1,0:T(8,128)(2,1)}, bf16[4,2,128,256]{3,2,1,0:T(8,128)(2,1)}, u32[]{:S(2)}, u32[]{:S(2)}) collective-permute-start(bf16[4,2,128,256]{3,2,1,0:T(8,128)(2,1)} %get-tuple-element.152), channel_id=1, source_target_pairs={{0,8},{4,12},{8,0},{12,4},{1,9},{5,13},{9,1},{13,5},{2,10},{6,14},... | collective-permute-start | bytes 1572872 | tf_op jit(solution)/shard_map/ppermute | solution.py:16
  68.9 46.4 %collective-permute-start.2 = (bf16[4,2,128,256]{3,2,1,0:T(8,128)(2,1)S(1)}, bf16[4,2,128,256]{3,2,1,0:T(8,128)(2,1)}, u32[]{:S(2)}, u32[]{:S(2)}) collective-permute-start(bf16[4,2,128,256]{3,2,1,0:T(8,128)(2,1)S(1)} %get-tuple-element.151), channel_id=1, source_target_pairs={{0,12},{4,0},{8,4},{12,8},{1,13},{5,1},{9,5},{13,9},{2,14},{6,2},{... | collective-permute-start | bytes 1572872 | tf_op jit(solution)/shard_map/ppermute | solution.py:16
  79.4 36.0 %copy-start.3 = (bf16[4,2,128,256]{3,2,1,0:T(8,128)(2,1)}, bf16[4,2,128,256]{3,2,1,0:T(8,128)(2,1)S(1)}, u32[]{:S(2)}) copy-start(bf16[4,2,128,256]{3,2,1,0:T(8,128)(2,1)S(1)} %collective-permute-done) | copy-start | bytes 1572868
  117.7 1.2 copy-start.1
where the time goes:
time: 133 us
  waiting for transfers between devices  58.5 us (44%)
  local copies, waits for them, and re-layouts  50.6 us (38%)
  starting transfers between devices  8.11 us (6%)
  other arithmetic  7.99 us (6%)
  matrix products  7.18 us (5%)
    ppermute x3, waiting for transfers between devices, passed_along(): return lax.ppermute(value, axis, pairs)  42.4 us
    unnamed x21, local copies, waits for them, and re-layouts  30.3 us
    all_to_all x1, waiting for transfers between devices, on_device(): lax.all_to_all(page_pool, 'tensor', split_axis=3, concat_axis=2, tiled=True)  16 us
    all_to_all x2, local copies, waits for them, and re-layouts, on_device(): lax.all_to_all(page_pool, 'tensor', split_axis=3, concat_axis=2, tiled=True)  11 us
    dot_general x3, matrix products, absorb(): jnp.einsum('kgqc,ckd->kgqd', weights.astype(jnp.bfloat16), values, prefer...  5.31 us
    all_to_all x1, starting transfers between devices, on_device(): lax.all_to_all(page_pool, 'tensor', split_axis=3, concat_axis=2, tiled=True)  4.34 us
    ppermute x3, starting transfers between devices, passed_along(): return lax.ppermute(value, axis, pairs)  3.78 us
  transfers between devices with their start and end apart: 4, of which 4 were waited for; matrix products, arithmetic and copies ran while one was open for 4% of the time, Pallas kernels for 0%

commit v1 on v0

--- a/solution.py
+++ b/solution.py
@@ -8,6 +8,22 @@
 KV_HEADS = 8
 HEAD_DIM = 128
 NEG_FILL = -1e30
+
+
+def exchange_in_pairs(shard, axis, split, join):
+    ways, here = (lax.axis_size(axis), lax.axis_index(axis))
+    width = shard.shape[split] // ways
+    dims = list(shard.shape)
+    dims[split] = width
+    height = dims[join]
+    dims[join] = height * ways
+    full = jnp.zeros(dims, shard.dtype)
+    for mask in range(ways):
+        part = lax.dynamic_slice_in_dim(shard, (here ^ mask) * width, width, axis=split)
+        if mask:
+            part = lax.ppermute(part, axis, [(d, d ^ mask) for d in range(ways)])
+        full = lax.dynamic_update_slice_in_dim(full, part, (here ^ mask) * height, axis=join)
+    return full
 
 
 def passed_along(value, axis, steps):
@@ -61,7 +77,7 @@
     slot_cap = (page_count + span_count - 1) // span_count + 1
     own_offsets = lax.dynamic_index_in_dim(offsets, reader, 0, keepdims=False)
     own_length = lax.dynamic_index_in_dim(prefix_len, reader, 0, keepdims=False)
-    source = lax.all_to_all(page_pool, "tensor", split_axis=3, concat_axis=2, tiled=True)
+    source = exchange_in_pairs(page_pool, "tensor", 3, 2)
     payload = pack_pages(source, offsets, slots, reader, replicas, span_count, slot_cap)
     arrivals = []
     for distance in range(1, span_count + 1):

time: 133 us -> 98.6 us (0.74)
  the two profiles are of different devices: /device:TPU:9 before, /device:TPU:0 now
where the time goes in v1:
time: 98.6 us; the launch traced here: 98 us
  waiting for transfers between devices  46.7 us (47%)
  local copies, waits for them, and re-layouts  20.4 us (21%)
  other arithmetic  13.9 us (14%)
  starting transfers between devices  8.48 us (9%)
  matrix products  8.03 us (8%)
    ppermute x3, waiting for transfers between devices, passed_along(): return lax.ppermute(value, axis, pairs)  42.5 us
    ppermute x3, starting transfers between devices, passed_along(): return lax.ppermute(value, axis, pairs)  5.43 us
    dot_general x3, matrix products, absorb(): jnp.einsum('kgqc,ckd->kgqd', weights.astype(jnp.bfloat16), values, prefer...  5.32 us
    unnamed x28, local copies, waits for them, and re-layouts  5.27 us
    ppermute x3, waiting for transfers between devices, exchange_in_pairs(): part = lax.ppermute(part, axis, [(d, d ^ mask) for d in range(ways)])  4.17 us
    reduce_sum x3, other arithmetic, absorb(): run_sum = run_sum * rescale + jnp.sum(weights, axis=-1)  3.86 us
    dynamic_update_slice x3, local copies, waits for them, and re-layouts, exchange_in_pairs(): lax.dynamic_update_slice_in_dim(full, part, (here ^ mask) * height, axis=...  3.08 us
    ppermute x3, starting transfers between devices, exchange_in_pairs(): part = lax.ppermute(part, axis, [(d, d ^ mask) for d in range(ways)])  3.06 us
  transfers between devices with their start and end apart: 6, of which 4 were waited for; matrix products, arithmetic and copies ran while one was open for 17% of the time, Pallas kernels for 0%

profile of v1, /device:TPU:0, one launch (start us, length us, event | category | flops | bytes accessed | tf_op | source)
XLA Modules:
  0.0 98.0 jit_solution(15418257391009124400)
XLA Ops:
  0.2 1.3 %copy-done.2 = bf16[12,2,32,1024]{3,2,1,0:T(8,128)(2,1)S(1)} copy-done((bf16[12,2,32,1024]{3,2,1,0:T(8,128)(2,1)S(1)}, bf16[12,2,32,1024]{3,2,1,0:T(8,128)(2,1)}, u32[]{:S(2)}) %copy-start.2) | copy-done | bytes 1572888
  1.4 1.1 %constant_dynamic-slice_fusion.2 = (bf16[12,2,32,256]{3,2,1,0:T(8,128)(2,1)S(1)}, bf16[12,2,32,256]{3,2,1,0:T(8,128)(2,1)}, bf16[12,2,128,256]{3,2,1,0:T(8,128)(2,1)S(1)}, bf16[12,2,32,256]{3,2,1,0:T(8,128)(2,1)}) fusion(bf16[12,2,32,1024]{3,2,1,0:T(8,128)(2,1)S(1)} %copy-done.2, s32[]{:T(128)S(6)} %select_n.113, s32[]{:T(128)S(6)} %select_n.109, ...), kind=kLoop, calls=%fused_computation.61 | loop fusion | bytes 3145748 | tf_op jit(solution)/shard_map/dynamic_slice | solution.py:22
  2.5 2.4 %collective-permute-start.2 = (bf16[12,2,32,256]{3,2,1,0:T(8,128)(2,1)S(1)}, bf16[12,2,32,256]{3,2,1,0:T(8,128)(2,1)}, u32[]{:S(2)}, u32[]{:S(2)}) collective-permute-start(bf16[12,2,32,256]{3,2,1,0:T(8,128)(2,1)S(1)} %get-tuple-element.135), channel_id=1, source_target_pairs={{0,3},{1,2},{2,1},{3,0},{4,7},{5,6},{6,5},{7,4},{8,11},{9,10},{10,... | collective-permute-start | bytes 1179656 | tf_op jit(solution)/shard_map/ppermute | solution.py:24
  4.9 0.7 collective-permute-start
  5.8 0.5 fusion.31
  6.4 0.5 compare_and_fusion.2
  6.9 0.6 gather_fusion.2
  7.5 0.6 gather_fusion.3
  8.7 0.6 iota_compare_fusion
  9.3 0.5 compare_and_fusion.1
  9.8 1.5 %fusion.37 = (bf16[1,1,128,256]{3,2,1,0:T(8,128)(2,1)}, bf16[1,1,128,256]{3,2,1,0:T(8,128)(2,1)S(1)}) fusion(bf16[1,2,128,256]{3,2,1,0:T(8,128)(2,1)} %param.11), kind=kLoop, calls=%fused_computation.88 | loop fusion | bytes 262144 | tf_op jit(solution)/shard_map/slice | solution.py:96
  11.3 0.7 copy.59
  12.1 1.3 %copy.36 = bf16[1,128,2048]{1,2,0:T(8,128)(2,1)S(1)} copy(bf16[1,128,2048]{2,1,0:T(8,128)(2,1)} %param.10) | data formatting | bytes 1048576 | tf_op args[0]
  13.4 1.2 %fusion.38 = (f32[2,8,128]{2,1,0:T(8,128)S(1)}, f32[2,8,128,128]{2,3,1,0:T(8,128)S(1)}) fusion(bf16[128,2,128,1]{0,2,3,1:T(8,128)(2,1)} %bitcast.95, bf16[128,2,8,128]{0,3,2,1:T(8,128)(2,1)S(1)} %bitcast.89, pred[128,128]{0,1:T(8,128)(4,1)} %iota_compare_fusion), kind=kOutput, calls=%fused_computation.89 | convolution fusion | flops 67893248 | bytes 1662976 | tf_op jit(solution)/shard_map/qkgd,ckd->kgqc/dot_general | solution.py:103
  14.6 0.6 copy-done.6
  15.2 0.6 pad_clamp_fusion.1
  15.8 0.6 pad_clamp_fusion
  16.4 1.5 %fusion.21 = f32[2,8,128]{2,1,0:T(8,128)} fusion(f32[2,8,128,128]{2,3,1,0:T(8,128)S(1)} %get-tuple-element.146, f32[2,8,128]{2,1,0:T(8,128)S(1)} %broadcast_maximum_fusion, pred[128,128]{0,1:T(8,128)(4,1)} %iota_compare_fusion), kind=kLoop, calls=%fused_computation.38 | loop fusion | flops 784384 | bytes 1081344 | tf_op jit(solution)/shard_map/reduce_sum | solution.py:41
  17.9 1.0 %constant_dynamic-update-slice_fusion.2 = bf16[12,2,128,256]{3,2,1,0:T(8,128)(2,1)S(1)} fusion(bf16[12,2,128,256]{3,2,1,0:T(8,128)(2,1)S(1)} %get-tuple-element.137, bf16[12,2,32,256]{3,2,1,0:T(8,128)(2,1)} %collective-permute-done, s32[]{:T(128)S(6)} %select_n.110), kind=kLoop, calls=%fused_computation.64 | loop fusion | bytes 786436 | tf_op jit(solution)/shard_map/dynamic_update_slice | solution.py:25
  18.9 4.2 %collective-permute-done.1 = bf16[12,2,32,256]{3,2,1,0:T(8,128)(2,1)} collective-permute-done((bf16[12,2,32,256]{3,2,1,0:T(8,128)(2,1)}, bf16[12,2,32,256]{3,2,1,0:T(8,128)(2,1)}, u32[]{:S(2)}, u32[]{:S(2)}) %collective-permute-start.1) | collective-permute-done | bytes 393248 | tf_op jit(solution)/shard_map/ppermute | solution.py:24
  23.1 1.0 %constant_dynamic-update-slice_fusion.1 = bf16[12,2,128,256]{3,2,1,0:T(8,128)(2,1)S(1)} fusion(bf16[12,2,128,256]{3,2,1,0:T(8,128)(2,1)S(1)} %constant_dynamic-update-slice_fusion.2, bf16[12,2,32,256]{3,2,1,0:T(8,128)(2,1)} %collective-permute-done.1, s32[]{:T(128)S(6)} %select_n.112), kind=kLoop, calls=%fused_computation.62 | loop fusion | bytes 786436 | tf_op jit(solution)/shard_map/dynamic_update_slice | solution.py:25
  24.1 1.0 %constant_dynamic-update-slice_fusion = bf16[12,2,128,256]{3,2,1,0:T(8,128)(2,1)S(1)} fusion(bf16[12,2,128,256]{3,2,1,0:T(8,128)(2,1)S(1)} %constant_dynamic-update-slice_fusion.1, bf16[12,2,32,256]{3,2,1,0:T(8,128)(2,1)} %collective-permute-done.2, s32[]{:T(128)S(6)} %select_n.114), kind=kLoop, calls=%fused_computation.60 | loop fusion | bytes 786436 | tf_op jit(solution)/shard_map/dynamic_update_slice | solution.py:25
  25.2 2.0 %gather_fusion = bf16[12,2,128,256]{3,2,1,0:T(8,128)(2,1)} fusion(bf16[12,2,128,256]{3,2,1,0:T(8,128)(2,1)S(1)} %constant_dynamic-update-slice_fusion, s32[1024]{0:T(1024)} %pad_clamp_fusion.1), kind=kCustom, calls=%fused_computation.2 | custom fusion | bytes 3145776 | tf_op jit(solution)/shard_map/jit(_take)/gather | solution.py:59
  27.2 1.6 %broadcast_select_fusion = bf16[12,2,128,256]{3,2,1,0:T(8,128)(2,1)S(1)} fusion(bf16[12,2,128,256]{3,2,1,0:T(8,128)(2,1)} %gather_fusion, pred[12]{0:T(512)(128)(4,1)S(1)} %copy-done.10), kind=kLoop, calls=%fused_computation.29 | loop fusion | flops 786432 | bytes 3145740 | tf_op jit(solution)/shard_map/jit(_take)/select_n | solution.py:59
  28.8 1.2 %fusion.35 = (bf16[4,2,128,256]{3,2,1,0:T(8,128)(2,1)}, bf16[4,2,128,256]{3,2,1,0:T(8,128)(2,1)}, bf16[4,2,128,256]{3,2,1,0:T(8,128)(2,1)}) fusion(bf16[12,2,128,256]{3,2,1,0:T(8,128)(2,1)S(1)} %broadcast_select_fusion), kind=kLoop, calls=%fused_computation.86 | loop fusion | bytes 3145728 | tf_op jit(solution)/shard_map/slice | solution.py:84
  30.0 2.4 %collective-permute-start.3 = (bf16[4,2,128,256]{3,2,1,0:T(8,128)(2,1)}, bf16[4,2,128,256]{3,2,1,0:T(8,128)(2,1)S(1)}, u32[]{:S(2)}, u32[]{:S(2)}) collective-permute-start(bf16[4,2,128,256]{3,2,1,0:T(8,128)(2,1)} %get-tuple-element.132), channel_id=1, source_target_pairs={{0,4},{4,8},{8,12},{12,0},{1,5},{5,9},{9,13},{13,1},{2,6},{6,10},{... | collective-permute-start | bytes 1572872 | tf_op jit(solution)/shard_map/ppermute | solution.py:32
  32.4 2.0 %collective-permute-start.5 = (bf16[4,2,128,256]{3,2,1,0:T(8,128)(2,1)}, bf16[4,2,128,256]{3,2,1,0:T(8,128)(2,1)S(1)}, u32[]{:S(2)}, u32[]{:S(2)}) collective-permute-start(bf16[4,2,128,256]{3,2,1,0:T(8,128)(2,1)} %get-tuple-element.133), channel_id=1, source_target_pairs={{0,12},{4,0},{8,4},{12,8},{1,13},{5,1},{9,5},{13,9},{2,14},{6,2},{... | collective-permute-start | bytes 1572872 | tf_op jit(solution)/shard_map/ppermute | solution.py:32
  34.4 1.0 %collective-permute-start.4 = (bf16[4,2,128,256]{3,2,1,0:T(8,128)(2,1)}, bf16[4,2,128,256]{3,2,1,0:T(8,128)(2,1)}, u32[]{:S(2)}, u32[]{:S(2)}) collective-permute-start(bf16[4,2,128,256]{3,2,1,0:T(8,128)(2,1)} %get-tuple-element.134), channel_id=1, source_target_pairs={{0,8},{4,12},{8,0},{12,4},{1,9},{5,13},{9,1},{13,5},{2,10},{6,14},... | collective-permute-start | bytes 1572872 | tf_op jit(solution)/shard_map/ppermute | solution.py:32
  35.8 0.6 dynamic_slice.31
  36.6 1.5 %convolution_add_fusion = f32[2,8,128,128]{3,2,1,0:T(8,128)} fusion(bf16[128,2,128,1]{0,2,3,1:T(8,128)(2,1)S(1)} %bitcast.94, f32[2,8,128,128]{2,3,1,0:T(8,128)S(1)} %get-tuple-element.146, f32[2,8,128]{2,1,0:T(8,128)S(1)} %get-tuple-element.143, f32[2,8,128]{2,1,0:T(8,128)S(1)} %broadcast_maximum_fusion, pred[128,128]{0,1:T(8,128)(4,1)S(1)} %copy-done.3), kind=kOutput, calls=%fused_computation.30 | convolution fusion | flops 68157440 | bytes 2195456 | tf_op jit(solution)/shard_map/kgqc,ckd->kgqd/dot_general | solution.py:42
  38.1 9.3 %collective-permute-done.3 = bf16[4,2,128,256]{3,2,1,0:T(8,128)(2,1)S(1)} collective-permute-done((bf16[4,2,128,256]{3,2,1,0:T(8,128)(2,1)}, bf16[4,2,128,256]{3,2,1,0:T(8,128)(2,1)S(1)}, u32[]{:S(2)}, u32[]{:S(2)}) %collective-permute-start.3) | collective-permute-done | bytes 524320 | tf_op jit(solution)/shard_map/ppermute | solution.py:32
  47.4 10.1 %collective-permute-done.5 = bf16[4,2,128,256]{3,2,1,0:T(8,128)(2,1)S(1)} collective-permute-done((bf16[4,2,128,256]{3,2,1,0:T(8,128)(2,1)}, bf16[4,2,128,256]{3,2,1,0:T(8,128)(2,1)S(1)}, u32[]{:S(2)}, u32[]{:S(2)}) %collective-permute-start.5) | collective-permute-done | bytes 524320 | tf_op jit(solution)/shard_map/ppermute | solution.py:32
  57.5 23.1 %collective-permute-done.4 = bf16[4,2,128,256]{3,2,1,0:T(8,128)(2,1)} collective-permute-done((bf16[4,2,128,256]{3,2,1,0:T(8,128)(2,1)}, bf16[4,2,128,256]{3,2,1,0:T(8,128)(2,1)}, u32[]{:S(2)}, u32[]{:S(2)}) %collective-permute-start.4) | collective-permute-done | bytes 524320 | tf_op jit(solution)/shard_map/ppermute | solution.py:32
  80.6 1.2 %pad_maximum_fusion = bf16[3,4,2,128,256]{4,3,2,1,0:T(8,128)(2,1)S(1)} fusion(bf16[1,4,2,128,256]{4,3,2,1,0:T(8,128)(2,1)S(1)} %bitcast.93, bf16[1,4,2,128,256]{4,3,2,1,0:T(8,128)(2,1)} %bitcast.10, bf16[1,4,2,128,256]{4,3,2,1,0:T(8,128)(2,1)S(1)} %bitcast.92), kind=kLoop, calls=%fused_computation.28 | loop fusion | flops 1572864 | bytes 3145728 | tf_op jit(solution)/shard_map/stack | solution.py:85
  81.8 0.6 gather_fusion.1
  83.0 1.0 copy-done.1
  84.0 12.3 %while.15 = (s32[]{:T(128)}, f32[2,8,128]{2,1,0:T(8,128)S(1)}, f32[2,8,128]{2,1,0:T(8,128)S(1)}, f32[2,8,128,128]{3,2,1,0:T(8,128)S(1)}, s32[2]{0:T(128)S(1)}, /...) while((s32[]{:T(128)}, f32[2,8,128]{2,1,0:T(8,128)S(1)}, ...), condition=%wide.region_8.10_spmd.clone, body=%wide.region_5.9_spmd.clone.sunk | while | flops 551031808 | bytes 16910468 | solution.py:127
  84.0 0.6 dynamic_slice.56
  84.5 1.3 %fusion.50 = pred[512]{0:T(512)(128)(4,1)S(1)} fusion(s32[]{:T(128)} %get-tuple-element.241, s32[]{:T(128)} %bitcast.88), kind=kLoop, calls=%fused_computation.22.clone.1 | loop fusion | flops 1024 | bytes 520 | tf_op jit(solution)/shard_map/while/body/eval_jaxpr/lt | solution.py:123
  86.2 0.8 bitcast_reduce_fusion.2
  87.0 1.2 %fusion.51 = f32[2,8,128]{2,1,0:T(8,128)S(1)} fusion(f32[2,512,128,8]{2,1,3,0:T(8,128)S(1)} %get-tuple-element.212, f32[2,8,128]{2,1,0:T(8,128)S(1)} %max.5, pred[512]{0:T(512)(128)(4,1)S(1)} %fusion.50), kind=kLoop, calls=%fused_computation.11.clone.1 | loop fusion | flops 5240832 | bytes 4211200 | tf_op jit(solution)/shard_map/while/body/eval_jaxpr/reduce_sum | solution.py:41
  88.2 1.9 %fusion.52 = f32[2,8,128,128]{3,2,1,0:T(8,128)S(1)} fusion(f32[2,512,128,8]{2,1,3,0:T(8,128)S(1)} %get-tuple-element.212, f32[2,8,128]{2,1,0:T(8,128)S(1)} %max.5, pred[512]{0:T(512)(128)(4,1)S(1)} %fusion.50, f32[2,8,128,128]{3,2,1,0:T(8,128)S(1)} %get-tuple-element.229, f32[2,8,128]{2,1,0:T(8,128)S(1)} %get-tuple-element.214, ...), kind=kOutput, calls=%fused_computation.15.clone.1 | convolution fusion | flops 274202624 | bytes 6570496 | tf_op jit(solution)/shard_map/while/body/eval_jaxpr/kgqc,ckd->kgqd/dot_general | solution.py:42
  90.1 0.6 dynamic_slice.56
  90.7 1.3 %fusion.50 = pred[512]{0:T(512)(128)(4,1)S(1)} fusion(s32[]{:T(128)} %get-tuple-element.241, s32[]{:T(128)} %bitcast.88), kind=kLoop, calls=%fused_computation.22.clone.1 | loop fusion | flops 1024 | bytes 520 | tf_op jit(solution)/shard_map/while/body/eval_jaxpr/lt | solution.py:123
  92.4 0.8 bitcast_reduce_fusion.2
  93.1 1.2 %fusion.51 = f32[2,8,128]{2,1,0:T(8,128)S(1)} fusion(f32[2,512,128,8]{2,1,3,0:T(8,128)S(1)} %get-tuple-element.212, f32[2,8,128]{2,1,0:T(8,128)S(1)} %max.5, pred[512]{0:T(512)(128)(4,1)S(1)} %fusion.50), kind=kLoop, calls=%fused_computation.11.clone.1 | loop fusion | flops 5240832 | bytes 4211200 | tf_op jit(solution)/shard_map/while/body/eval_jaxpr/reduce_sum | solution.py:41
  94.3 1.9 %fusion.52 = f32[2,8,128,128]{3,2,1,0:T(8,128)S(1)} fusion(f32[2,512,128,8]{2,1,3,0:T(8,128)S(1)} %get-tuple-element.212, f32[2,8,128]{2,1,0:T(8,128)S(1)} %max.5, pred[512]{0:T(512)(128)(4,1)S(1)} %fusion.50, f32[2,8,128,128]{3,2,1,0:T(8,128)S(1)} %get-tuple-element.229, f32[2,8,128]{2,1,0:T(8,128)S(1)} %get-tuple-element.214, ...), kind=kOutput, calls=%fused_computation.15.clone.1 | convolution fusion | flops 274202624 | bytes 6570496 | tf_op jit(solution)/shard_map/while/body/eval_jaxpr/kgqc,ckd->kgqd/dot_general | solution.py:42
  97.0 1.0 %convert_element_type.35 = bf16[1,128,2048]{2,1,0:T(8,128)(2,1)} reshape(bf16[128,2,8,128]{3,2,1,0:T(8,128)(2,1)S(1)} %copy.45) | data formatting | bytes 1048576 | tf_op jit(solution)/shard_map/convert_element_type | solution.py:131
  (57 shorter events, 3.5 us)
Async XLA Ops:
  0.0 7.4 %copy-start = (s32[4,8]{1,0:T(4,128)S(1)}, s32[4,8]{1,0:T(4,128)}, u32[]{:S(2)}) copy-start(s32[4,8]{1,0:T(4,128)} %param.14) | copy-start | bytes 388
  0.0 1.4 %copy-start.2 = (bf16[12,2,32,1024]{3,2,1,0:T(8,128)(2,1)S(1)}, bf16[12,2,32,1024]{3,2,1,0:T(8,128)(2,1)}, u32[]{:S(2)}) copy-start(bf16[12,2,32,1024]{3,2,1,0:T(8,128)(2,1)} %param.12) | copy-start | bytes 4718596
  1.4 4.2 %copy-start.5 = (s32[4,8]{1,0:T(4,128)S(1)}, s32[4,8]{1,0:T(4,128)}, u32[]{:S(2)}) copy-start(s32[4,8]{1,0:T(4,128)} %param.13) | copy-start | bytes 388
  2.5 21.6 %collective-permute-start.2 = (bf16[12,2,32,256]{3,2,1,0:T(8,128)(2,1)S(1)}, bf16[12,2,32,256]{3,2,1,0:T(8,128)(2,1)}, u32[]{:S(2)}, u32[]{:S(2)}) collective-permute-start(bf16[12,2,32,256]{3,2,1,0:T(8,128)(2,1)S(1)} %get-tuple-element.135), channel_id=1, source_target_pairs={{0,3},{1,2},{2,1},{3,0},{4,7},{5,6},{6,5},{7,4},{8,11},{9,10},{10,... | collective-permute-start | bytes 1179656 | tf_op jit(solution)/shard_map/ppermute | solution.py:24
  4.9 13.0 %collective-permute-start = (bf16[12,2,32,256]{3,2,1,0:T(8,128)(2,1)}, bf16[12,2,32,256]{3,2,1,0:T(8,128)(2,1)}, u32[]{:S(2)}, u32[]{:S(2)}) collective-permute-start(bf16[12,2,32,256]{3,2,1,0:T(8,128)(2,1)} %get-tuple-element.136), channel_id=1, source_target_pairs={{0,1},{1,0},{2,3},{3,2},{4,5},{5,4},{6,7},{7,6},{8,9},{9,8},{10,11... | collective-permute-start | bytes 1179656 | tf_op jit(solution)/shard_map/ppermute | solution.py:24
  5.6 17.5 %collective-permute-start.1 = (bf16[12,2,32,256]{3,2,1,0:T(8,128)(2,1)}, bf16[12,2,32,256]{3,2,1,0:T(8,128)(2,1)}, u32[]{:S(2)}, u32[]{:S(2)}) collective-permute-start(bf16[12,2,32,256]{3,2,1,0:T(8,128)(2,1)} %get-tuple-element.138), channel_id=1, source_target_pairs={{0,2},{1,3},{2,0},{3,1},{4,6},{5,7},{6,4},{7,5},{8,10},{9,11},{10,... | collective-permute-start | bytes 1179656 | tf_op jit(solution)/shard_map/ppermute | solution.py:24
  14.6 0.6 copy-start.6
  25.2 2.0 %copy-start.10 = (pred[12]{0:T(512)(128)(4,1)S(1)}, pred[12]{0:T(512)(128)(4,1)}, u32[]{:S(2)}) copy-start(pred[12]{0:T(512)(128)(4,1)} %compare_and_fusion.1) | copy-start | bytes 40
  28.8 7.0 %copy-start.11 = (s32[4]{0:T(128)S(1)}, s32[4]{0:T(128)}, u32[]{:S(2)}) copy-start(s32[4]{0:T(128)} %param.15) | copy-start | bytes 52
  28.8 7.6 %copy-start.4 = (bf16[1,1,128,256]{3,2,1,0:T(8,128)(2,1)S(1)}, bf16[1,1,128,256]{3,2,1,0:T(8,128)(2,1)}, u32[]{:S(2)}) copy-start(bf16[1,1,128,256]{3,2,1,0:T(8,128)(2,1)} %get-tuple-element.141) | copy-start | bytes 196612
  28.8 7.7 %copy-start.7 = (f32[2,8,128]{2,1,0:T(8,128)S(1)}, f32[2,8,128]{2,1,0:T(8,128)}, u32[]{:S(2)}) copy-start(f32[2,8,128]{2,1,0:T(8,128)} %copy-done.6) | copy-start | bytes 24580
  28.8 7.7 %copy-start.8 = (f32[2,8,128]{2,1,0:T(8,128)S(1)}, f32[2,8,128]{2,1,0:T(8,128)}, u32[]{:S(2)}) copy-start(f32[2,8,128]{2,1,0:T(8,128)} %fusion.21) | copy-start | bytes 24580
  28.8 7.7 %copy-start.3 = (pred[128,128]{0,1:T(8,128)(4,1)S(1)}, pred[128,128]{0,1:T(8,128)(4,1)}, u32[]{:S(2)}) copy-start(pred[128,128]{0,1:T(8,128)(4,1)} %iota_compare_fusion) | copy-start | bytes 49156
  30.0 17.4 %collective-permute-start.3 = (bf16[4,2,128,256]{3,2,1,0:T(8,128)(2,1)}, bf16[4,2,128,256]{3,2,1,0:T(8,128)(2,1)S(1)}, u32[]{:S(2)}, u32[]{:S(2)}) collective-permute-start(bf16[4,2,128,256]{3,2,1,0:T(8,128)(2,1)} %get-tuple-element.132), channel_id=1, source_target_pairs={{0,4},{4,8},{8,12},{12,0},{1,5},{5,9},{9,13},{13,1},{2,6},{6,10},{... | collective-permute-start | bytes 1572872 | tf_op jit(solution)/shard_map/ppermute | solution.py:32
  32.4 25.1 %collective-permute-start.5 = (bf16[4,2,128,256]{3,2,1,0:T(8,128)(2,1)}, bf16[4,2,128,256]{3,2,1,0:T(8,128)(2,1)S(1)}, u32[]{:S(2)}, u32[]{:S(2)}) collective-permute-start(bf16[4,2,128,256]{3,2,1,0:T(8,128)(2,1)} %get-tuple-element.133), channel_id=1, source_target_pairs={{0,12},{4,0},{8,4},{12,8},{1,13},{5,1},{9,5},{13,9},{2,14},{6,2},{... | collective-permute-start | bytes 1572872 | tf_op jit(solution)/shard_map/ppermute | solution.py:32
  34.4 46.2 %collective-permute-start.4 = (bf16[4,2,128,256]{3,2,1,0:T(8,128)(2,1)}, bf16[4,2,128,256]{3,2,1,0:T(8,128)(2,1)}, u32[]{:S(2)}, u32[]{:S(2)}) collective-permute-start(bf16[4,2,128,256]{3,2,1,0:T(8,128)(2,1)} %get-tuple-element.134), channel_id=1, source_target_pairs={{0,8},{4,12},{8,0},{12,4},{1,9},{5,13},{9,1},{13,5},{2,10},{6,14},... | collective-permute-start | bytes 1572872 | tf_op jit(solution)/shard_map/ppermute | solution.py:32
  81.8 0.6 copy-start.9
  82.7 1.2 %copy-start.1 = (f32[2,8,128,128]{3,2,1,0:T(8,128)S(1)}, f32[2,8,128,128]{3,2,1,0:T(8,128)}, u32[]{:S(2)}) copy-start(f32[2,8,128,128]{3,2,1,0:T(8,128)} %convolution_add_fusion) | copy-start | bytes 3145732
